TPU v7x, 256 devices: a whole 4x4x8 slice. The times are simulated.
256 devices in a mesh: fsdp: 16 (over z_hi, x), tensor: 16 (over z_lo, y, core).
Axes of the slice: x: 4, y: 4, z: 8 (z_hi: 4, z_lo: 2; z = z_hi * 2 + z_lo), core: 2. Of those that a mesh axis runs over, the one named last changes fastest.
Arguments:
- tokens: bfloat16 [8192, 3072], P('fsdp'), may hold values from -6 to 6
- weights: bfloat16 [3072, 4, 4096], P('fsdp', None, 'tensor'), may hold values from -0.109375 to 0.109375
- direction: bfloat16 [3072, 4, 4096], P('fsdp', None, 'tensor'), may hold values from -0.109375 to 0.109375
- precision: float32 [3072], replicated, may hold values from 0.25 to 4
Outputs:
- ggn: float32 [3072, 4, 4096], P('fsdp', None, 'tensor')
All inputs are finite; a program needn't handle non-finite values.
Results may differ from a plain program's by a relative error of at most 0.015.
Values may be sent and summed in bfloat16 or wider, within the bound.
No kernel may reach another device: no remote copies, remote signals or barrier semaphores. Data moves between devices by JAX's collectives and lax.ppermute only.
A program may use at most 128 MiB of HBM per device.

v0:
```python
import jax
import jax.numpy as jnp
from jax import lax
from jax.sharding import PartitionSpec as P

HEAD = 128
PATCHES = 256


def layer_norm(rows):
    mean_row = jnp.mean(rows, -1, keepdims=True)
    centred = rows - mean_row
    spread = jnp.mean(centred * centred, -1, keepdims=True)
    return centred * lax.rsqrt(spread + 1e-06)


def attend(queries, key_rows, value_rows):
    query_norm = layer_norm(queries)
    key_norm = layer_norm(key_rows)
    score_scale = queries.shape[-1] ** (-0.5)
    scores = (
        jnp.einsum("bqhe,bkhe->bhqk", query_norm, key_norm, precision=lax.Precision.HIGHEST)
        * score_scale
    )
    exponent = jnp.exp(scores)
    attn_weights = exponent / jnp.sum(exponent, -1, keepdims=True)
    return jnp.einsum("bhqk,bkhe->bqhe", attn_weights, value_rows, precision=lax.Precision.HIGHEST)


def cross_rows(left, right):
    return lax.dot_general(
        left, right, (((1,), (1,)), ((), ())), preferred_element_type=jnp.float32
    )


def over_tokens(left, right):
    return lax.dot_general(
        left, right, (((0,), (0,)), ((), ())), preferred_element_type=jnp.float32
    )


def body(tokens, weights, direction, precision):
    model_width = tokens.shape[1]
    local_rows = tokens.shape[0]
    head_cols = weights.shape[2]
    normed = layer_norm(tokens.astype(jnp.float32)).astype(jnp.bfloat16)
    full_weights = lax.all_gather(weights, "fsdp", axis=0, tiled=True)
    full_direction = lax.all_gather(direction, "fsdp", axis=0, tiled=True)
    in_weights = full_weights[:, 0:3, :].reshape(model_width, 3 * head_cols)
    in_direction = full_direction[:, 0:3, :].reshape(model_width, 3 * head_cols)
    projected = jnp.dot(normed, in_weights, preferred_element_type=jnp.float32).astype(jnp.bfloat16)
    tangent_in = jnp.dot(normed, in_direction, preferred_element_type=jnp.float32).astype(
        jnp.bfloat16
    )

    def to_heads(block):
        return block.astype(jnp.float32).reshape(
            local_rows // PATCHES, PATCHES, 3, head_cols // HEAD, HEAD
        )

    primal = to_heads(projected)
    tangent_heads = to_heads(tangent_in)
    primal_args = (primal[:, :, 0], primal[:, :, 1], primal[:, :, 2])
    tangent_args = (tangent_heads[:, :, 0], tangent_heads[:, :, 1], tangent_heads[:, :, 2])
    mixed, mixed_dot = jax.jvp(attend, primal_args, tangent_args)
    mixed_rows = mixed.reshape(local_rows, head_cols).astype(jnp.bfloat16)
    tangent_out = mixed_dot.reshape(local_rows, head_cols).astype(jnp.bfloat16)
    out_weights = full_weights[:, 3, :]
    out_direction = full_direction[:, 3, :]
    partial_sum = cross_rows(tangent_out, out_weights) + cross_rows(mixed_rows, out_direction)
    output_dot = lax.psum(partial_sum.astype(jnp.bfloat16), "tensor").astype(jnp.float32)
    cotangent = (precision * output_dot).astype(jnp.bfloat16)
    share_rows = model_width // lax.axis_size("fsdp")
    back_rows = jnp.dot(cotangent, out_weights, preferred_element_type=jnp.float32)
    back_rows = back_rows.reshape(local_rows // PATCHES, PATCHES, head_cols // HEAD, HEAD)
    primal_out, pullback = jax.vjp(attend, *primal_args)
    gradients = pullback(back_rows)
    stacked = jnp.stack(gradients, axis=2).reshape(local_rows, 3 * head_cols).astype(jnp.bfloat16)
    return lax.psum_scatter(
        jnp.concatenate(
            [
                over_tokens(normed, stacked).reshape(
                    lax.axis_size("fsdp") * share_rows, 3, head_cols
                ),
                over_tokens(cotangent, mixed_rows)[:, None, :],
            ],
            axis=1,
        ).astype(jnp.bfloat16),
        "fsdp",
        scatter_dimension=0,
        tiled=True,
    ).astype(jnp.float32)


def solution(mesh):
    return jax.shard_map(
        body,
        mesh=mesh,
        in_specs=(P("fsdp", None), P("fsdp", None, "tensor"), P("fsdp", None, "tensor"), P()),
        out_specs=P("fsdp", None, "tensor"),
        check_vma=False,
    )
```

profile of v0, /device:TPU:1, one launch (start us, length us, event | category | flops | bytes accessed | tf_op | source)
XLA Modules:
  0.0 533.6 jit_solution(97903180383077813)
XLA Ops:
  8.1 2.4 convert_reduce_fusion
  11.4 92.9 %all-gather.5.cloned.1.call-done = bf16[3072,4,256]{2,1,0:T(4,128)(2,1)} async-done(((bf16[192,4,256]{2,1,0:T(4,128)(2,1)}), bf16[3072,4,256]{2,1,0:T(4,128)(2,1)}) %all-gather.5.cloned.1.call-update) | async-done | bytes 6291472 | tf_op jit(solution)/shard_map/all_gather | solution.py:47
  104.3 10.1 %copy.106 = bf16[3072,3,256]{0,2,1:T(8,128)(2,1)} copy(bf16[3072,3,256]{2,1,0:T(4,128)(2,1)} %bitcast.153) | data formatting | bytes 9437184
  114.4 5.9 %convolution_convert_fusion.2 = bf16[512,768]{1,0:T(8,128)(2,1)} fusion(bf16[3072,768]{0,1:T(8,128)(2,1)} %bitcast.157, bf16[512,3072]{1,0:T(8,128)(2,1)S(1)} %copy-done.1, f32[512]{0:T(512)S(1)} %add_rsqrt_fusion, f32[512]{0:T(512)S(1)} %broadcast_multiply_fusion.4), kind=kOutput, calls=%fused_computation.16 | convolution fusion | flops 2422603776 | bytes 8654848 | tf_op jit(solution)/shard_map/dot_general | solution.py:51
  120.3 2.0 reshape.137
  123.6 78.6 %all-gather.3.cloned.1.call-done = bf16[3072,4,256]{2,1,0:T(4,128)(2,1)} async-done(((bf16[192,4,256]{2,1,0:T(4,128)(2,1)}), bf16[3072,4,256]{2,1,0:T(4,128)(2,1)}) %all-gather.3.cloned.1.call-update) | async-done | bytes 6291472 | tf_op jit(solution)/shard_map/all_gather | solution.py:48
  202.2 10.1 %copy.105 = bf16[3072,3,256]{0,2,1:T(8,128)(2,1)} copy(bf16[3072,3,256]{2,1,0:T(4,128)(2,1)} %bitcast.154) | data formatting | bytes 9437184
  212.3 5.9 %convolution_convert_fusion.3 = bf16[512,768]{1,0:T(8,128)(2,1)S(1)} fusion(bf16[3072,768]{0,1:T(8,128)(2,1)} %bitcast.158, bf16[512,3072]{1,0:T(8,128)(2,1)} %param.4, f32[512]{0:T(512)S(1)} %add_rsqrt_fusion, f32[512]{0:T(512)S(1)} %broadcast_multiply_fusion.4), kind=kOutput, calls=%fused_computation.17 | convolution fusion | flops 2422603776 | bytes 8654848 | tf_op jit(solution)/shard_map/dot_general | solution.py:52
  218.4 2.1 copy.58
  220.5 1.3 reshape.139
  222.3 1.2 fusion.65
  223.4 2.4 fusion.11
  225.8 2.3 fusion.42
  230.5 1.3 fusion.66
  231.8 1.6 fusion.13
  233.6 6.2 %slice.48 = bf16[3072,1,256]{2,1,0:T(2,128)(2,1)S(1)} slice(bf16[3072,4,256]{2,1,0:T(4,128)(2,1)} %all-gather.5.cloned.1.call-done), slice={[0:3072], [3:4], [0:256]} | slice | bytes 3145728 | tf_op jit(solution)/shard_map/slice | solution.py:68
  242.6 3.4 slice.49
  246.0 2.7 add_convert_fusion
  248.8 6.4 %copy.109 = bf16[3072,1,256]{0,2,1:T(8,128)(2,1)S(1)} copy(bf16[3072,1,256]{2,1,0:T(2,128)(2,1)} %copy-done) | data formatting | bytes 3145728 | tf_op jit(solution)/shard_map/dot_general | solution.py:74
  255.3 129.1 %all-reduce.2.cloned.1.call-done = bf16[512,3072]{1,0:T(8,128)(2,1)} async-done(((bf16[512,3072]{1,0:T(8,128)(2,1)}), bf16[512,3072]{1,0:T(8,128)(2,1)}) %all-reduce.2.cloned.1.call-update) | async-done | bytes 3145744 | tf_op jit(solution)/shard_map/psum | solution.py:71
  384.4 2.6 multiply_convert_fusion
  388.2 1.6 multiply_reduce_fusion
  389.8 1.3 fusion.12
  391.1 2.2 fusion.4
  394.3 1.5 fusion.58
  397.3 3.3 copy.83
  400.6 3.1 convert_element_type.64
  403.7 2.3 copy.84
  406.0 4.8 convolution_convert_fusion
  410.8 3.2 pad_maximum_fusion
  414.0 110.8 %reduce-scatter.2.cloned.1.call-done = bf16[192,4,256]{2,0,1:T(8,128)(2,1)} async-done(((bf16[3072,4,256]{2,0,1:T(8,128)(2,1)}), bf16[192,4,256]{2,0,1:T(8,128)(2,1)}) %reduce-scatter.2.cloned.1.call-update) | async-done | bytes 393232 | tf_op jit(solution)/shard_map/reduce_scatter | solution.py:79
  524.8 2.2 copy.86
  (62 shorter events, 13.2 us)
Async XLA Ops:
  6.5 3.9 copy-start.1
  6.5 97.8 %all-gather.5.cloned.1.call-start = ((), (), s32[]{:S(2)}) async-start(), calls=%async_computation.2 | async-start | bytes 6684672 | tf_op jit(solution)/shard_map/all_gather | solution.py:47
  7.3 194.9 %all-gather.3.cloned.1.call-start = ((), (), s32[]{:S(2)}) async-start(), calls=%async_computation.1 | async-start | bytes 6684672 | tf_op jit(solution)/shard_map/all_gather | solution.py:48
  8.0 376.4 %all-reduce.2.cloned.1.call-start = ((), (), s32[]{:S(2)}) async-start(), calls=%async_computation.3 | async-start | bytes 6291456 | tf_op jit(solution)/shard_map/psum | solution.py:71
  123.4 89.0 %copy-start.6 = (bf16[2,256,3,2,128]{1,4,3,0,2:T(8,128)(2,1)}, bf16[2,256,3,2,128]{1,4,3,0,2:T(8,128)(2,1)S(1)}, u32[]{:S(2)}) copy-start(bf16[2,256,3,2,128]{1,4,3,0,2:T(8,128)(2,1)S(1)} %copy.60) | copy-start | bytes 2359300
  223.4 4.7 copy-start.3
  229.3 1.2 copy-start.4
  229.3 2.5 copy-start.9
  233.6 8.0 %slice-start = ((s8[6291456]{0:T(1024)(128)(4,1)}), s8[4194304]{0:T(1024)(128)(4,1)S(1)}, s32[]{:S(2)}) async-start(s8[6291456]{0:T(1024)(128)(4,1)} %bitcast.155), calls=%async_computation.5 | async-start | bytes 8388608
  239.8 1.7 copy-start
  239.8 2.7 slice-start.1
  248.8 135.6 %copy-start.8 = (f32[3072]{0:T(1024)S(1)}, f32[3072]{0:T(1024)}, u32[]{:S(2)}) copy-start(f32[3072]{0:T(1024)} %param.7) | copy-start | bytes 36868
  248.8 276.1 %reduce-scatter.2.cloned.1.call-start = ((), (), s32[]{:S(2)}) async-start(), calls=%async_computation.4 | async-start | bytes 6684672 | tf_op jit(solution)/shard_map/reduce_scatter | solution.py:79
  386.9 1.2 copy-start.5
  396.3 9.7 %copy-start.2 = (bf16[512,3072]{1,0:T(8,128)(2,1)S(1)}, bf16[512,3072]{1,0:T(8,128)(2,1)}, u32[]{:S(2)}) copy-start(bf16[512,3072]{1,0:T(8,128)(2,1)} %param.4) | copy-start | bytes 9437188
  406.0 4.8 copy-start.7
Sparse Core Ops, SparseCore 0:
  9.8 94.4 all-gather.4
  106.7 95.4 all-gather.2
  248.9 135.4 all-reduce.1
  414.2 110.6 reduce-scatter.1
where the time goes:
time: 535 us; the launch traced here: 534 us
  waiting for transfers between devices  413 us (77%)
  local copies, waits for them, and re-layouts  55.8 us (10%)
  matrix products  38.9 us (7%)
  between operations  13.5 us (3%)
  other arithmetic  12.5 us (2%)
    psum x1, waiting for transfers between devices, body(): lax.psum(partial_sum.astype(jnp.bfloat16), 'tensor').astype(jnp.float32)  129 us
    reduce_scatter x1, waiting for transfers between devices, body(): lax.psum_scatter(jnp.concatenate([over_tokens(normed, stacked).reshape(la...  111 us
    all_gather x1, waiting for transfers between devices, body(): full_weights = lax.all_gather(weights, 'fsdp', axis=0, tiled=True)  92.9 us
    all_gather x1, waiting for transfers between devices, body(): full_direction = lax.all_gather(direction, 'fsdp', axis=0, tiled=True)  78.6 us
    unnamed x26, local copies, waits for them, and re-layouts  22.2 us
  transfers between devices with their start and end apart: 4, of which 4 were waited for; matrix products, arithmetic and copies ran while one was open for 5% of the time, Pallas kernels for 0%

commit v1 on v0

--- a/solution.py
+++ b/solution.py
@@ -68,7 +68,9 @@
     out_weights = full_weights[:, 3, :]
     out_direction = full_direction[:, 3, :]
     partial_sum = cross_rows(tangent_out, out_weights) + cross_rows(mixed_rows, out_direction)
-    output_dot = lax.psum(partial_sum.astype(jnp.bfloat16), "tensor").astype(jnp.float32)
+    output_dot = jnp.sum(lax.all_gather(partial_sum.astype(jnp.bfloat16), "tensor"), axis=0).astype(
+        jnp.float32
+    )
     cotangent = (precision * output_dot).astype(jnp.bfloat16)
     share_rows = model_width // lax.axis_size("fsdp")
     back_rows = jnp.dot(cotangent, out_weights, preferred_element_type=jnp.float32)

time: 535 us -> 661 us (1.24)
  waiting for transfers between devices: 413 us -> 535 us
  other arithmetic: 12.5 us -> 30.3 us
  local copies, waits for them, and re-layouts: 55.8 us -> 46.5 us
    all_gather x0 -> x1, waiting for transfers between devices: none -> 251 us  [body(): lax.all_gather(partial_sum.astype(jnp.bfloat16), 'tensor')]
    psum x1 -> x0, waiting for transfers between devices: 129 us -> none  [body(): lax.psum(partial_sum.astype(jnp.bfloat16), 'tensor').astype(jnp.float32)]
    reduce_sum x0 -> x1, other arithmetic: none -> 18.6 us  [body(): jnp.sum(lax.all_gather(partial_sum.astype(jnp.bfloat16), 'tensor'), axis=0)]
    all_gather x1, waiting for transfers between devices: 78.6 us -> 92.4 us  [body(): full_direction = lax.all_gather(direction, 'fsdp', axis=0, tiled=True)]
    all_gather x1, waiting for transfers between devices: 92.9 us -> 80.3 us  [body(): full_weights = lax.all_gather(weights, 'fsdp', axis=0, tiled=True)]
    unnamed x26 -> x22, local copies, waits for them, and re-layouts: 22.2 us -> 22.5 us
  transfers between devices with their start and end apart: 4 -> 4, of which waited for: 4 -> 4; matrix products, arithmetic and copies ran while one was open for 5% -> 4% of each run, Pallas kernels for 0% -> 0%
where the time goes in v1:
time: 661 us; the launch traced here: 660 us
  waiting for transfers between devices  535 us (81%)
  local copies, waits for them, and re-layouts  46.5 us (7%)
  matrix products  35.2 us (5%)
  other arithmetic  30.3 us (5%)
  between operations  13.5 us (2%)
    all_gather x1, waiting for transfers between devices, body(): lax.all_gather(partial_sum.astype(jnp.bfloat16), 'tensor')  251 us
    reduce_scatter x1, waiting for transfers between devices, body(): lax.psum_scatter(jnp.concatenate([over_tokens(normed, stacked).reshape(la...  109 us
    all_gather x1, waiting for transfers between devices, body(): full_direction = lax.all_gather(direction, 'fsdp', axis=0, tiled=True)  92.4 us
    all_gather x1, waiting for transfers between devices, body(): full_weights = lax.all_gather(weights, 'fsdp', axis=0, tiled=True)  80.3 us
    unnamed x22, local copies, waits for them, and re-layouts  22.5 us
    reduce_sum x1, other arithmetic, body(): jnp.sum(lax.all_gather(partial_sum.astype(jnp.bfloat16), 'tensor'), axis=0)  18.6 us
  transfers between devices with their start and end apart: 4, of which 4 were waited for; matrix products, arithmetic and copies ran while one was open for 4% of the time, Pallas kernels for 0%

profile of v1, /device:TPU:1, one launch (start us, length us, event | category | flops | bytes accessed | tf_op | source)
XLA Modules:
  0.0 660.2 jit_solution(18267985723765091871)
XLA Ops:
  8.1 2.5 convert_reduce_fusion
  11.9 92.4 %all-gather.5.cloned.1.call-done = bf16[3072,4,256]{2,1,0:T(4,128)(2,1)} async-done(((bf16[192,4,256]{2,1,0:T(4,128)(2,1)}), bf16[3072,4,256]{2,1,0:T(4,128)(2,1)}) %all-gather.5.cloned.1.call-update) | async-done | bytes 6291472 | tf_op jit(solution)/shard_map/all_gather | solution.py:48
  104.3 10.1 %copy.105 = bf16[3072,3,256]{0,2,1:T(8,128)(2,1)} copy(bf16[3072,3,256]{2,1,0:T(4,128)(2,1)} %bitcast.155) | data formatting | bytes 9437184
  114.4 5.9 convolution_convert_fusion.3
  121.8 80.3 %all-gather.7.cloned.1.call-done = bf16[3072,4,256]{2,1,0:T(4,128)(2,1)} async-done(((bf16[192,4,256]{2,1,0:T(4,128)(2,1)}), bf16[3072,4,256]{2,1,0:T(4,128)(2,1)}) %all-gather.7.cloned.1.call-update) | async-done | bytes 6291472 | tf_op jit(solution)/shard_map/all_gather | solution.py:47
  202.2 10.1 %copy.106 = bf16[3072,3,256]{0,2,1:T(8,128)(2,1)} copy(bf16[3072,3,256]{2,1,0:T(4,128)(2,1)} %bitcast.158) | data formatting | bytes 9437184
  212.3 5.9 convolution_convert_fusion.2
  218.4 2.1 copy.60
  220.5 1.3 reshape.167
  222.2 1.2 fusion.65
  223.4 1.7 fusion.42
  225.2 1.3 fusion.11
  226.5 1.1 fusion.23
  227.6 1.3 fusion.66
  230.0 6.4 slice.48
  236.5 1.0 fusion.6
  238.1 1.1 slice-done.1
  239.2 3.4 slice.49
  242.6 2.7 add_convert_fusion
  245.3 6.2 copy.109
  251.6 251.2 %all-gather.9.cloned.1.call-done = bf16[8192,3072]{1,0:T(8,128)(2,1)} async-done(((bf16[512,3072]{1,0:T(8,128)(2,1)}), bf16[8192,3072]{1,0:T(8,128)(2,1)}) %all-gather.9.cloned.1.call-update) | async-done | bytes 50331664 | tf_op jit(solution)/shard_map/all_gather | solution.py:71
  502.8 18.6 %reduce_sum.183 = bf16[512,3072]{1,0:T(8,128)(2,1)} reduce(bf16[16,512,3072]{2,1,0:T(8,128)(2,1)} %bitcast.154, bf16[]{:T(256)} %constant.30.clone.1), dimensions={0}, to_apply=%region_12.0 | reduce | flops 23592960 | bytes 53477376 | tf_op jit(solution)/shard_map/reduce_sum | solution.py:71
  521.3 2.6 multiply_convert_fusion
  525.1 1.3 fusion.12
  526.5 1.7 multiply_reduce_fusion
  528.1 1.0 fusion.4
  530.2 1.5 fusion.58
  532.2 1.3 copy.83
  534.2 4.9 convolution_convert_fusion
  539.1 3.2 pad_maximum_fusion
  542.3 109.2 %reduce-scatter.2.cloned.1.call-done = bf16[192,4,256]{2,0,1:T(8,128)(2,1)} async-done(((bf16[3072,4,256]{2,0,1:T(8,128)(2,1)}), bf16[192,4,256]{2,0,1:T(8,128)(2,1)}) %reduce-scatter.2.cloned.1.call-update) | async-done | bytes 393232 | tf_op jit(solution)/shard_map/reduce_scatter | solution.py:81
  651.5 2.2 copy.86
  (59 shorter events, 9.9 us)
Async XLA Ops:
  6.5 97.8 %all-gather.5.cloned.1.call-start = ((), (), s32[]{:S(2)}) async-start(), calls=%async_computation.1 | async-start | bytes 6684672 | tf_op jit(solution)/shard_map/all_gather | solution.py:48
  7.3 194.9 %all-gather.7.cloned.1.call-start = ((), (), s32[]{:S(2)}) async-start(), calls=%async_computation.2 | async-start | bytes 6684672 | tf_op jit(solution)/shard_map/all_gather | solution.py:47
  8.0 494.8 %all-gather.9.cloned.1.call-start = ((), (), s32[]{:S(2)}) async-start(), calls=%async_computation.4 | async-start | bytes 53477376 | tf_op jit(solution)/shard_map/all_gather | solution.py:71
  8.1 2.8 copy-start.1
  121.6 90.7 %copy-start.5 = (bf16[2,256,3,2,128]{1,4,3,0,2:T(8,128)(2,1)}, bf16[2,256,3,2,128]{1,4,3,0,2:T(8,128)(2,1)S(1)}, u32[]{:S(2)}) copy-start(bf16[2,256,3,2,128]{1,4,3,0,2:T(8,128)(2,1)S(1)} %copy.58) | copy-start | bytes 2359300
  222.2 3.0 copy-start.4
  223.4 5.5 copy-start.2
  228.9 1.0 copy-start.6
  230.0 8.1 %slice-start = ((s8[6291456]{0:T(1024)(128)(4,1)}), s8[4194304]{0:T(1024)(128)(4,1)S(1)}, s32[]{:S(2)}) async-start(s8[6291456]{0:T(1024)(128)(4,1)} %bitcast.156), calls=%async_computation.5 | async-start | bytes 8388608
  236.4 1.6 copy-start
  236.4 2.7 slice-start.1
  245.3 406.2 %reduce-scatter.2.cloned.1.call-start = ((), (), s32[]{:S(2)}) async-start(), calls=%async_computation.3 | async-start | bytes 6684672 | tf_op jit(solution)/shard_map/reduce_scatter | solution.py:81
  502.8 18.6 %copy-start.7 = (f32[3072]{0:T(1024)S(1)}, f32[3072]{0:T(1024)}, u32[]{:S(2)}) copy-start(f32[3072]{0:T(1024)} %param.7) | copy-start | bytes 36868
  523.9 1.2 copy-start.3
Sparse Core Ops, SparseCore 0:
  9.8 94.4 all-gather.4
  106.7 95.3 all-gather.6
  245.4 257.3 all-gather.8
  542.4 109.0 reduce-scatter.1
